TPU v7x, 32 devices: a whole 2x2x4 slice. The times are simulated.
32 devices in a mesh: pages: 8 (over y, x, core), mp: 4 (over z).
Axes of the slice: x: 2, y: 2, z: 4, core: 2. Of those that a mesh axis runs over, the one named last changes fastest.
Arguments:
- hidden_in: bfloat16 [2048, 1280], P('pages'), may hold values from -240 to 240
- w_qkv: bfloat16 [3, 1280, 1280], P(None, None, 'mp'), may hold values from -0.15625 to 0.15625
- w_out: bfloat16 [1280, 1280], replicated, may hold values from -0.15625 to 0.15625
- w_gate_up: bfloat16 [2, 1280, 5120], P(None, None, 'mp'), may hold values from -0.15625 to 0.15625
- w_down: bfloat16 [5120, 1280], P('mp'), may hold values from -0.078125 to 0.078125
- scale_qk: float32 [1280], replicated, may hold values from 0.4 to 1.6
- scale_gate_up: float32 [2, 5120], P(None, 'mp'), may hold values from 0.5 to 2
- eigen_rates: float32 [2, 1280], replicated, may hold values from 0.1 to 1
- cache_keys: bfloat16 [32, 128, 1280], P('pages'), may hold values from -6 to 6
- cache_values: bfloat16 [32, 128, 1280], P('pages'), may hold values from -6 to 6
- page_table: int32 [32], replicated, may hold values from 0 to 31, as said below
- request_group: int32 [8, 4], replicated, may hold values from 0 to 7
- suffix_len: int32 [8, 4], replicated, may hold values from 1 to 253, as said below
Outputs:
- hidden_out: bfloat16 [2048, 1280], P(('pages', 'mp'))
Inputs may be any that keep to these rules, and one draw needn't show every extreme that they name: `suffix_len`: the 4 lengths of one index of pages sum to at least 153 and at most 256, and to exactly 256 for at least one index. `page_table`: A permutation of the pool pages; the 4 pool pages of one index of pages hold prefix pages of 4 different groups.
All inputs are finite; a program needn't handle non-finite values.
Results may differ from a plain program's by a relative error of at most 0.013.
Values may be sent and summed in bfloat16 or wider, within the bound.
No kernel may reach another device: no remote copies, remote signals or barrier semaphores. Data moves between devices by JAX's collectives and lax.ppermute only.
A program may use at most 128 MiB of HBM per device.

v0:
```python
import math
import jax
import jax.numpy as jnp
from jax import lax
from jax.sharding import PartitionSpec as P

HEADS = 20
GROUPS = 8
EPSILON = 1e-06


def rms_rows(values_in):
    return values_in * lax.rsqrt(jnp.mean(values_in * values_in, axis=-1, keepdims=True) + EPSILON)


def head_norm(values_in, scale_vec, head_count):
    row_count, model_width = values_in.shape
    per_head = values_in.reshape(row_count, head_count, model_width // head_count)
    normed = per_head * lax.rsqrt(jnp.mean(per_head * per_head, axis=-1, keepdims=True) + EPSILON)
    return normed.reshape(row_count, model_width) * scale_vec[None, :]


def rotate(values_in, position, head_count):
    row_count, model_width = values_in.shape
    head_dim = model_width // head_count
    half_dim = head_dim // 2
    frequency = jnp.exp(
        jnp.arange(half_dim).astype(jnp.float32) * (-2.0 * math.log(10000.0) / head_dim)
    )
    rotation = position.astype(jnp.float32)[:, None] * frequency[None, :]
    cosine_table = jnp.cos(rotation)[:, None, :]
    sine_table = jnp.sin(rotation)[:, None, :]
    per_head = values_in.reshape(row_count, head_count, head_dim)
    lower_half = per_head[:, :, :half_dim]
    upper_half = per_head[:, :, half_dim:]
    turned = jnp.concatenate(
        [
            lower_half * cosine_table - upper_half * sine_table,
            upper_half * cosine_table + lower_half * sine_table,
        ],
        axis=-1,
    )
    return turned.reshape(row_count, model_width)


def slot_tables(suffix_len, request_group, slot_count):
    end_slots = jnp.cumsum(suffix_len, axis=1)
    start_slots = end_slots - suffix_len
    slot_ids = jnp.arange(slot_count)
    inside = (slot_ids[None, None, :] >= start_slots[:, :, None]) & (
        slot_ids[None, None, :] < end_slots[:, :, None]
    )
    request_ids = jnp.arange(suffix_len.shape[1])
    slot_valid = jnp.any(inside, axis=1)
    request = jnp.sum(jnp.where(inside, request_ids[None, :, None], 0), axis=1)
    offset = slot_ids[None, :] - jnp.sum(jnp.where(inside, start_slots[:, :, None], 0), axis=1)
    group_id = jnp.where(
        slot_valid, jnp.sum(jnp.where(inside, request_group[:, :, None], 0), axis=1), -1
    )
    return (slot_valid, request, offset, group_id)


def prefix_block(query_block, group_block, prefix_keys, prefix_values, key_group, score_scale):
    row_count, model_width = query_block.shape
    head_dim = model_width // HEADS
    query_heads = query_block.reshape(row_count, HEADS, head_dim)
    key_heads = prefix_keys.reshape(-1, HEADS, head_dim)
    value_heads = prefix_values.reshape(-1, HEADS, head_dim)
    scores = (
        jnp.einsum("qhd,khd->qhk", query_heads, key_heads, preferred_element_type=jnp.float32)
        * score_scale
    )
    allowed = group_block[:, None] == key_group[None, :]
    weights = jnp.where(allowed[:, None, :], jnp.exp(scores), 0.0)
    weight_sum = jnp.sum(weights, axis=-1)
    summed = jnp.einsum(
        "qhk,khd->qhd",
        weights.astype(jnp.bfloat16),
        value_heads,
        preferred_element_type=jnp.float32,
    )
    return (summed.reshape(row_count, model_width), weight_sum)


def shards_columns(
    hidden_in,
    w_qkv,
    w_out,
    w_gate_up,
    w_down,
    scale_qk,
    scale_gate_up,
    eigen_rates,
    cache_keys,
    cache_values,
    page_table,
    request_group,
    suffix_len,
):
    slot_count, model_width = hidden_in.shape
    head_dim = model_width // HEADS
    score_scale = 1.0 / math.sqrt(head_dim)
    mp_count = lax.axis_size("mp")
    mp_index = lax.axis_index("mp")
    own_rows = slot_count // mp_count
    row_first = mp_index * own_rows
    shard_index = lax.axis_index("pages")
    pages_here, page_len = (cache_keys.shape[0], cache_keys.shape[1])
    pool_pages = page_table.shape[0]
    prefix_pages = pool_pages // GROUPS
    slot_valid, request, offset, group_id = slot_tables(suffix_len, request_group, slot_count)
    live_shard = lax.dynamic_index_in_dim(slot_valid, shard_index, 0, keepdims=False)
    request_shard = lax.dynamic_index_in_dim(request, shard_index, 0, keepdims=False)
    offset_shard = lax.dynamic_index_in_dim(offset, shard_index, 0, keepdims=False)
    position_shard = prefix_pages * page_len + offset_shard
    live_own = lax.dynamic_slice_in_dim(live_shard, row_first, own_rows, 0)
    request_own = lax.dynamic_slice_in_dim(request_shard, row_first, own_rows, 0)
    offset_own = lax.dynamic_slice_in_dim(offset_shard, row_first, own_rows, 0)
    position_own = lax.dynamic_slice_in_dim(position_shard, row_first, own_rows, 0)
    state_in = rms_rows(hidden_in.astype(jnp.float32)).astype(jnp.bfloat16)
    projected = jnp.einsum(
        "sd,jdc->jsc", state_in, w_qkv, preferred_element_type=jnp.float32
    ).astype(jnp.bfloat16)
    columns = lax.all_gather(projected, "mp", axis=2, tiled=True)
    query_raw = lax.dynamic_slice_in_dim(columns[0], row_first, own_rows, 0)
    key_raw, value_rows = (columns[1], columns[2])
    queries = head_norm(
        rotate(query_raw.astype(jnp.float32), position_own, HEADS), scale_qk, HEADS
    ).astype(jnp.bfloat16)
    keys_new = head_norm(
        rotate(key_raw.astype(jnp.float32), position_shard, HEADS), scale_qk, HEADS
    ).astype(jnp.bfloat16)
    query_heads = queries.reshape(own_rows, HEADS, head_dim)
    scores = (
        jnp.einsum(
            "qhd,khd->hqk",
            query_heads,
            keys_new.reshape(slot_count, HEADS, head_dim),
            preferred_element_type=jnp.float32,
        )
        * score_scale
    )
    allowed = (
        (request_own[:, None] == request_shard[None, :])
        & (offset_shard[None, :] <= offset_own[:, None])
        & live_own[:, None]
        & live_shard[None, :]
    )
    weights = jnp.where(allowed[None], jnp.exp(scores), 0.0)
    suffix_total = jnp.sum(weights, axis=-1)
    suffix_sum = jnp.einsum(
        "hqk,khd->qhd",
        weights.astype(jnp.bfloat16),
        value_rows.reshape(slot_count, HEADS, head_dim),
        preferred_element_type=jnp.float32,
    )
    physical = shard_index * pages_here + jnp.arange(pages_here, dtype=jnp.int32)
    matches = page_table[:, None] == physical[None, :]
    logical = jnp.sum(
        jnp.where(matches, jnp.arange(pool_pages, dtype=jnp.int32)[:, None], 0), axis=0
    )
    key_group = jnp.repeat(logical // prefix_pages, page_len)
    prefix_keys = head_norm(
        cache_keys.reshape(pages_here * page_len, model_width).astype(jnp.float32), scale_qk, HEADS
    ).astype(jnp.bfloat16)
    prefix_values = cache_values.reshape(pages_here * page_len, model_width)
    gathered = lax.all_gather(queries, "pages", axis=0, tiled=True)
    gathered_group = lax.dynamic_slice_in_dim(group_id, row_first, own_rows, 1).reshape(-1)
    row_count = own_rows * lax.axis_size("pages")
    block_rows = row_count if row_count <= 512 else math.gcd(row_count, 512)

    def attend_block(block_first):
        query_block = lax.dynamic_slice_in_dim(gathered, block_first, block_rows, 0)
        group_block = lax.dynamic_slice_in_dim(gathered_group, block_first, block_rows, 0)
        return prefix_block(
            query_block, group_block, prefix_keys, prefix_values, key_group, score_scale
        )

    block_starts = jnp.arange(row_count // block_rows, dtype=jnp.int32) * block_rows
    summed, weight_sum = lax.map(attend_block, block_starts)
    prefix_sum, prefix_total = lax.psum_scatter(
        (summed.reshape(row_count, model_width), weight_sum.reshape(row_count, HEADS)),
        "pages",
        scatter_dimension=0,
        tiled=True,
    )
    denominator = suffix_total.T + prefix_total + (1.0 - live_own.astype(jnp.float32))[:, None]
    mixed = (suffix_sum + prefix_sum.reshape(own_rows, HEADS, head_dim)) / denominator[:, :, None]
    attention = mixed.reshape(own_rows, model_width).astype(jnp.bfloat16)
    projected_out = jnp.dot(
        lax.all_gather(attention, "mp", axis=0, tiled=True),
        w_out,
        preferred_element_type=jnp.float32,
    )
    residual_in = state_in.astype(jnp.float32)
    state_mid = rms_rows(
        residual_in + eigen_rates[0][None, :] * (rms_rows(projected_out) - residual_in)
    ).astype(jnp.bfloat16)
    state_own = lax.dynamic_slice_in_dim(state_mid, row_first, own_rows, 0)
    gate_up = jnp.einsum("sd,jdf->jsf", state_mid, w_gate_up, preferred_element_type=jnp.float32)
    hidden = (
        jax.nn.silu(scale_gate_up[0][None, :] * gate_up[0])
        * (scale_gate_up[1][None, :] * gate_up[1])
    ).astype(jnp.bfloat16)
    feed_sum = lax.psum_scatter(
        jnp.dot(hidden, w_down, preferred_element_type=jnp.float32),
        "mp",
        scatter_dimension=0,
        tiled=True,
    )
    middle = state_own.astype(jnp.float32)
    result = rms_rows(middle + eigen_rates[1][None, :] * (rms_rows(feed_sum) - middle))
    return (live_own.astype(jnp.float32)[:, None] * result).astype(jnp.bfloat16)


def shards_heads(
    hidden_in,
    w_qkv,
    w_out,
    w_gate_up,
    w_down,
    scale_qk,
    scale_gate_up,
    eigen_rates,
    cache_keys,
    cache_values,
    page_table,
    request_group,
    suffix_len,
):
    slot_count, model_width = hidden_in.shape
    head_dim = model_width // HEADS
    score_scale = 1.0 / math.sqrt(head_dim)
    mp_count = lax.axis_size("mp")
    mp_index = lax.axis_index("mp")
    local_heads = HEADS // mp_count
    local_width = local_heads * head_dim
    own_rows = slot_count // mp_count
    row_first = mp_index * own_rows
    shard_index = lax.axis_index("pages")
    pages_here, page_len = (cache_keys.shape[0], cache_keys.shape[1])
    pool_pages = page_table.shape[0]
    prefix_pages = pool_pages // GROUPS
    slot_valid, request, offset, group_id = slot_tables(suffix_len, request_group, slot_count)
    live_shard = lax.dynamic_index_in_dim(slot_valid, shard_index, 0, keepdims=False)
    request_shard = lax.dynamic_index_in_dim(request, shard_index, 0, keepdims=False)
    offset_shard = lax.dynamic_index_in_dim(offset, shard_index, 0, keepdims=False)
    position_shard = prefix_pages * page_len + offset_shard
    live_own = lax.dynamic_slice_in_dim(live_shard, row_first, own_rows, 0)
    scale_local = lax.dynamic_slice_in_dim(scale_qk, mp_index * local_width, local_width, 0)
    state_in = rms_rows(hidden_in.astype(jnp.float32)).astype(jnp.bfloat16)
    projected = jnp.einsum(
        "sd,jdc->jsc", state_in, w_qkv, preferred_element_type=jnp.float32
    ).astype(jnp.bfloat16)
    queries = head_norm(
        rotate(projected[0].astype(jnp.float32), position_shard, local_heads),
        scale_local,
        local_heads,
    ).astype(jnp.bfloat16)
    keys_new = head_norm(
        rotate(projected[1].astype(jnp.float32), position_shard, local_heads),
        scale_local,
        local_heads,
    ).astype(jnp.bfloat16)
    value_rows = projected[2]
    gathered = lax.all_gather(queries, "pages", axis=0, tiled=True)
    scores = (
        jnp.einsum(
            "qhd,khd->hqk",
            queries.reshape(slot_count, local_heads, head_dim),
            keys_new.reshape(slot_count, local_heads, head_dim),
            preferred_element_type=jnp.float32,
        )
        * score_scale
    )
    allowed = (
        (request_shard[:, None] == request_shard[None, :])
        & (offset_shard[None, :] <= offset_shard[:, None])
        & live_shard[:, None]
        & live_shard[None, :]
    )
    weights = jnp.where(allowed[None], jnp.exp(scores), 0.0)
    suffix_total = jnp.sum(weights, axis=-1)
    suffix_sum = jnp.einsum(
        "hqk,khd->qhd",
        weights.astype(jnp.bfloat16),
        value_rows.reshape(slot_count, local_heads, head_dim),
        preferred_element_type=jnp.float32,
    )
    physical = shard_index * pages_here + jnp.arange(pages_here, dtype=jnp.int32)
    matches = page_table[:, None] == physical[None, :]
    logical = jnp.sum(
        jnp.where(matches, jnp.arange(pool_pages, dtype=jnp.int32)[:, None], 0), axis=0
    )
    key_group = jnp.repeat(logical // prefix_pages, page_len)
    cache_local = lax.dynamic_slice_in_dim(cache_keys, mp_index * local_width, local_width, 2)
    prefix_keys = head_norm(
        cache_local.reshape(pages_here * page_len, local_width).astype(jnp.float32),
        scale_local,
        local_heads,
    ).astype(jnp.bfloat16)
    prefix_values = lax.dynamic_slice_in_dim(
        cache_values, mp_index * local_width, local_width, 2
    ).reshape(pages_here * page_len, local_width)
    gathered_group = group_id.reshape(-1)
    row_count = gathered.shape[0]
    query_heads = gathered.reshape(row_count, local_heads, head_dim)
    key_heads = prefix_keys.reshape(-1, local_heads, head_dim)
    value_heads = prefix_values.reshape(-1, local_heads, head_dim)
    prefix_scores = (
        jnp.einsum("qhd,khd->qhk", query_heads, key_heads, preferred_element_type=jnp.float32)
        * score_scale
    )
    prefix_allowed = gathered_group[:, None] == key_group[None, :]
    prefix_weights = jnp.where(prefix_allowed[:, None, :], jnp.exp(prefix_scores), 0.0)
    weight_sum = jnp.sum(prefix_weights, axis=-1)
    summed = jnp.einsum(
        "qhk,khd->qhd",
        prefix_weights.astype(jnp.bfloat16),
        value_heads,
        preferred_element_type=jnp.float32,
    )
    prefix_sum, prefix_total = lax.psum_scatter(
        (summed.reshape(row_count, local_width), weight_sum),
        "pages",
        scatter_dimension=0,
        tiled=True,
    )
    denominator = suffix_total.T + prefix_total + (1.0 - live_shard.astype(jnp.float32))[:, None]
    mixed = (suffix_sum + prefix_sum.reshape(slot_count, local_heads, head_dim)) / denominator[
        :, :, None
    ]
    attention_local = mixed.reshape(slot_count, local_width).astype(jnp.bfloat16)
    attention = lax.all_gather(attention_local, "mp", axis=1, tiled=True)
    projected_out = jnp.dot(attention, w_out, preferred_element_type=jnp.float32)
    residual_in = state_in.astype(jnp.float32)
    state_mid = rms_rows(
        residual_in + eigen_rates[0][None, :] * (rms_rows(projected_out) - residual_in)
    ).astype(jnp.bfloat16)
    state_own = lax.dynamic_slice_in_dim(state_mid, row_first, own_rows, 0)
    gate_up = jnp.einsum("sd,jdf->jsf", state_mid, w_gate_up, preferred_element_type=jnp.float32)
    hidden = (
        jax.nn.silu(scale_gate_up[0][None, :] * gate_up[0])
        * (scale_gate_up[1][None, :] * gate_up[1])
    ).astype(jnp.bfloat16)
    feed_sum = lax.psum_scatter(
        jnp.dot(hidden, w_down, preferred_element_type=jnp.float32),
        "mp",
        scatter_dimension=0,
        tiled=True,
    )
    middle = state_own.astype(jnp.float32)
    result = rms_rows(middle + eigen_rates[1][None, :] * (rms_rows(feed_sum) - middle))
    return (live_own.astype(jnp.float32)[:, None] * result).astype(jnp.bfloat16)


def solution(mesh):
    shards = shards_heads if HEADS % mesh.shape["mp"] == 0 else shards_columns
    return jax.shard_map(
        shards,
        mesh=mesh,
        in_specs=(
            P("pages", None),
            P(None, None, "mp"),
            P(),
            P(None, None, "mp"),
            P("mp", None),
            P(),
            P(None, "mp"),
            P(),
            P("pages", None, None),
            P("pages", None, None),
            P(),
            P(),
            P(),
        ),
        out_specs=P(("pages", "mp"), None),
        check_vma=False,
    )
```

profile of v0, /device:TPU:0, one launch (start us, length us, event | category | flops | bytes accessed | tf_op | source)
XLA Modules:
  0.0 206.2 jit_solution(12084083910439738020)
XLA Ops:
  6.5 0.0 copy-start
  6.5 0.0 all-gather.2.cloned.1.call-start
  6.6 0.9 reduce_window_sum.11
  7.4 0.8 sub.37
  8.2 0.8 select_reduce_fusion.2
  9.0 1.3 fusion.9
  10.3 2.8 %fusion.16 = bf16[3,256,320]{1,2,0:T(8,128)(2,1)S(1)} fusion(bf16[3,1280,320]{1,2,0:T(8,128)(2,1)} %param.14, bf16[256,1280]{1,0:T(8,128)(2,1)} %param.13, f32[256]{0:T(256)S(1)} %add_rsqrt_fusion.5), kind=kOutput, calls=%fused_computation.29 | convolution fusion | flops 630374400 | bytes 3605504 | tf_op jit(solution)/shard_map/sd,jdc->jsc/dot_general | solution.py:252
  13.2 0.7 fusion.46
  13.9 0.2 multiply_cosine_fusion
  14.1 0.7 multiply_subtract_fusion
  14.9 0.8 fusion.33
  15.7 0.8 dynamic_slice.33
  16.4 1.7 fusion.30
  18.2 0.0 all-gather.2.cloned.1.call-update
  18.2 0.0 reduce-scatter.6.cloned.1.call-start
  18.3 0.1 mul.315
  18.3 0.1 fusion.44
  18.4 2.4 %constant_dynamic-slice_fusion = (bf16[4,128,320]{2,1,0:T(8,128)(2,1)}, bf16[4,128,320]{2,1,0:T(8,128)(2,1)}) fusion(bf16[4,128,1280]{2,1,0:T(8,128)(2,1)} %param.21, s32[]{:T(128)S(6)} %select_n.65, bf16[4,128,1280]{2,1,0:T(8,128)(2,1)} %param.22), kind=kLoop, calls=%fused_computation.90 | loop fusion | bytes 1310724 | tf_op jit(solution)/shard_map/dynamic_slice | solution.py:296
  20.9 1.9 copy.39
  22.8 2.1 copy.35
  24.9 2.2 %reshape.336 = f32[512,5,64]{0,2,1:T(8,128)} reshape(f32[4,128,320]{1,0,2:T(4,128)} %copy.35) | data formatting | bytes 1310720 | tf_op jit(solution)/shard_map/convert_element_type | solution.py:298
  27.1 1.9 copy.33
  29.0 1.9 reshape_reshape.3
  30.9 0.0 copy-done.6
  30.9 0.2 select_reduce_fusion.3
  31.0 1.2 multiply_reduce_fusion.2
  32.2 0.1 broadcast_bitcast_fusion
  32.3 1.6 broadcast_compare_fusion
  33.9 11.8 %all-gather.2.cloned.1.call-done = bf16[2048,320]{0,1:T(8,128)(2,1)} async-done(((bf16[256,320]{0,1:T(8,128)(2,1)}), bf16[2048,320]{0,1:T(8,128)(2,1)}) %all-gather.2.cloned.1.call-update) | async-done | bytes 1310736 | tf_op jit(solution)/shard_map/all_gather | solution.py:266
  45.8 11.8 %fusion = (f32[2048,5]{0,1:T(8,128)}, f32[5,512,2048]{2,1,0:T(8,128)}) fusion(pred[2048,512]{0,1:T(8,128)(4,1)} %broadcast_compare_fusion, bf16[2048,5,64]{0,2,1:T(8,128)(2,1)} %bitcast.93, f32[512,5,64]{0,2,1:T(8,128)} %reshape.336, f32[5,64]{1,0:T(8,128)S(1)} %mul.315, f32[512,5]{0,1:T(8,128)S(1)} %add_rsqrt_fusion), kind=kOutput, calls=%fused_computation.1 | convolution fusion | flops 687298560 | bytes 24038656 | tf_op jit(solution)/shard_map/qhd,khd->qhk/dot_general | solution.py:311
  57.5 0.0 reduce-scatter.6.cloned.1.call-update
  57.6 0.0 reduce-scatter.4.cloned.1.call-start
  57.6 12.5 %fusion.2 = f32[5,64,2048]{2,1,0:T(8,128)} fusion(bf16[512,5,64]{0,2,1:T(8,128)(2,1)} %reshape_reshape.3, f32[5,512,2048]{2,1,0:T(8,128)} %get-tuple-element.24, pred[2048,512]{0,1:T(8,128)(4,1)} %broadcast_compare_fusion), kind=kOutput, calls=%fused_computation.3 | convolution fusion | flops 686817280 | bytes 24969216 | tf_op jit(solution)/shard_map/qhk,khd->qhd/dot_general | solution.py:317
  70.1 0.0 reduce-scatter.4.cloned.1.call-update
  70.1 0.0 reduce-scatter.8.cloned.1.call-start
  70.2 1.0 multiply_reduce_fusion.5
  71.2 0.0 copy-done.3
  71.2 0.0 copy-done.4
  71.3 0.2 and_and_fusion
  71.5 2.4 %fusion.47 = (f32[5,256]{1,0:T(8,128)S(1)}, bf16[5,256,256]{1,2,0:T(8,128)(2,1)}) fusion(f32[256,5,32]{0,2,1:T(8,128)} %get-tuple-element.16, f32[256,5,32]{0,2,1:T(8,128)S(1)} %get-tuple-element.15, f32[256,5]{0,1:T(8,128)S(1)} %add_rsqrt_fusion.1, f32[5,64]{1,0:T(8,128)S(1)} %mul.315, f32[256,5,64]{0,2,1:T(8,128)} %fusion.33, ...), kind=kOutput, calls=%fused_computation.115 | convolution fusion | flops 43744000 | bytes 1387776 | tf_op jit(solution)/shard_map/qhd,khd->hqk/dot_general | solution.py:268
  73.9 17.0 %reduce-scatter.6.cloned.1.call-done = f32[256,5]{0,1:T(8,128)} async-done(((f32[2048,5]{0,1:T(8,128)}), f32[256,5]{0,1:T(8,128)}) %reduce-scatter.6.cloned.1.call-update) | async-done | bytes 5136 | tf_op jit(solution)/shard_map/reduce_scatter | solution.py:323
  90.9 0.7 fusion.37
  91.6 46.7 %reduce-scatter.4.cloned.1.call-done = f32[256,320]{0,1:T(8,128)} async-done(((f32[2048,320]{0,1:T(8,128)}), f32[256,320]{0,1:T(8,128)}) %reduce-scatter.4.cloned.1.call-update) | async-done | bytes 327696 | tf_op jit(solution)/shard_map/reduce_scatter | solution.py:323
  138.3 1.6 fusion.19
  140.0 18.1 %all_gather.7 = bf16[256,1280]{0,1:T(8,128)(2,1)S(1)} all-gather(bf16[256,320]{0,1:T(8,128)(2,1)S(1)} %bitcast.87), channel_id=1, replica_groups=mesh['pages'=8,'mp'=4] {'mp'}, dimensions={1}, use_global_device_ids=true | all-gather | bytes 819200 | tf_op jit(solution)/shard_map/all_gather | solution.py:334
  158.0 0.0 copy-done
  158.1 1.1 multiply_reduce_fusion.1
  159.2 0.0 copy-done.1
  159.2 0.5 multiply_reduce_fusion
  159.7 0.4 multiply_convert_fusion
  160.1 0.0 slice-done
  160.1 0.0 slice-done.1
  160.1 0.0 copy-start.2
  160.2 0.0 copy-start.5
  160.2 1.9 convolution_bitcast_fusion
  162.0 0.0 copy-done.2
  162.0 0.3 copy-done.5
  162.3 2.3 %fusion.20 = f32[256,1280]{1,0:T(8,128)} fusion(bf16[1280,1280]{1,0:T(8,128)(2,1)S(1)} %copy-done.5, f32[2,256,1280]{2,1,0:T(8,128)S(1)} %convolution_bitcast_fusion, f32[1280]{0:T(1024)S(1)} %get-tuple-element.8, f32[1280]{0:T(1024)S(1)} %get-tuple-element.7), kind=kOutput, calls=%fused_computation.34 | convolution fusion | flops 841482240 | bytes 7219200 | tf_op jit(solution)/shard_map/dot_general | solution.py:347
  164.6 0.0 reduce-scatter.8.cloned.1.call-update
  164.7 0.1 fusion.39
  164.7 30.6 %reduce-scatter.8.cloned.1.call-done = f32[64,1280]{1,0:T(8,128)} async-done(((f32[256,1280]{1,0:T(8,128)}), f32[64,1280]{1,0:T(8,128)}) %reduce-scatter.8.cloned.1.call-update) | async-done | bytes 327696 | tf_op jit(solution)/shard_map/reduce_scatter | solution.py:346
  195.3 1.1 multiply_reduce_fusion.4
  196.4 1.3 multiply_reduce_fusion.3
  197.7 1.9 multiply_convert_fusion.3
  (29 shorter events, 0.3 us)
Async XLA Ops:
  6.5 151.5 %copy-start = (bf16[1280,1280]{1,0:T(8,128)(2,1)S(1)}, bf16[1280,1280]{1,0:T(8,128)(2,1)}, u32[]{:S(2)}) copy-start(bf16[1280,1280]{1,0:T(8,128)(2,1)} %param.15) | copy-start | bytes 9830404
  6.5 39.2 %all-gather.2.cloned.1.call-start = ((), (), s32[]{:S(2)}) async-start(), calls=%async_computation.3 | async-start | bytes 1474560 | tf_op jit(solution)/shard_map/all_gather | solution.py:266
  18.2 72.7 %reduce-scatter.6.cloned.1.call-start = ((), (), s32[]{:S(2)}) async-start(), calls=%async_computation.5 | async-start | bytes 73728 | tf_op jit(solution)/shard_map/reduce_scatter | solution.py:323
  24.9 6.0 %copy-start.6 = (s32[32]{0:T(128)S(1)}, s32[32]{0:T(128)}, u32[]{:S(2)}) copy-start(s32[32]{0:T(128)} %param.23) | copy-start | bytes 388
  57.6 80.8 %reduce-scatter.4.cloned.1.call-start = ((), (), s32[]{:S(2)}) async-start(), calls=%async_computation.4 | async-start | bytes 2949120 | tf_op jit(solution)/shard_map/reduce_scatter | solution.py:323
  70.1 1.1 copy-start.3
  70.1 1.1 copy-start.4
  70.1 125.2 %reduce-scatter.8.cloned.1.call-start = ((), (), s32[]{:S(2)}) async-start(), calls=%async_computation.6 | async-start | bytes 1638400 | tf_op jit(solution)/shard_map/reduce_scatter | solution.py:346
  138.3 21.8 %slice-start = ((s8[6553600]{0:T(1024)(128)(4,1)}), s8[4194304]{0:T(1024)(128)(4,1)S(1)}, s32[]{:S(2)}) async-start(s8[6553600]{0:T(1024)(128)(4,1)} %bitcast.82), calls=%async_computation.7 | async-start | bytes 8388608
  158.0 1.1 copy-start.1
  158.0 2.1 %slice-start.1 = ((s8[6553600]{0:T(1024)(128)(4,1)}), s8[2359296]{0:T(1024)(128)(4,1)S(1)}, s32[]{:S(2)}) async-start(s8[6553600]{0:T(1024)(128)(4,1)} %bitcast.82), calls=%async_computation.8 | async-start | bytes 4718592
  160.1 1.9 copy-start.2
  160.2 2.2 %copy-start.5 = (bf16[1280,1280]{1,0:T(8,128)(2,1)S(1)}, bf16[1280,1280]{1,0:T(8,128)(2,1)}, u32[]{:S(2)}) copy-start(bf16[1280,1280]{1,0:T(8,128)(2,1)} %param.17) | copy-start | bytes 9830404
Sparse Core Ops, SparseCore 0:
  18.3 27.4 all-gather.1
  57.7 33.2 reduce-scatter.5
  94.6 43.6 reduce-scatter.3
  164.8 30.4 reduce-scatter.7
where the time goes:
time: 207 us; the launch traced here: 206 us
  waiting for transfers between devices  106 us (51%)
  matrix products  36.4 us (18%)
  blocking collectives  18.1 us (9%)
  other arithmetic  17.5 us (8%)
  local copies, waits for them, and re-layouts  14.4 us (7%)
  between operations  13.4 us (6%)
    reduce_scatter x2, waiting for transfers between devices, shards_heads(): lax.psum_scatter((summed.reshape(row_count, local_width), weight_sum), 'p...  63.7 us
    reduce_scatter x1, waiting for transfers between devices, shards_heads(): lax.psum_scatter(jnp.dot(hidden, w_down, preferred_element_type=jnp.float...  30.6 us
    all_gather x1, blocking collectives, shards_heads(): attention = lax.all_gather(attention_local, 'mp', axis=1, tiled=True)  18.1 us
    dot_general x1, matrix products, shards_heads(): jnp.einsum('qhk,khd->qhd', prefix_weights.astype(jnp.bfloat16), value_hea...  12.5 us
    all_gather x1, waiting for transfers between devices, shards_heads(): gathered = lax.all_gather(queries, 'pages', axis=0, tiled=True)  11.8 us
    dot_general x1, matrix products, shards_heads(): jnp.einsum('qhd,khd->qhk', query_heads, key_heads, preferred_element_type...  11.8 us
    convert_element_type x2, local copies, waits for them, and re-layouts, shards_heads(): cache_local.reshape(pages_here * page_len, local_width).astype(jnp.float32)  4.28 us
    reduce_sum x4, other arithmetic, rms_rows(): jnp.mean(values_in * values_in, axis=-1, keepdims=True) + EPSILON  4.16 us
  transfers between devices with their start and end apart: 4, of which 4 were waited for; matrix products, arithmetic and copies ran while one was open for 16% of the time, Pallas kernels for 0%

commit v1 on v0

--- a/solution.py
+++ b/solution.py
@@ -263,7 +263,14 @@
         local_heads,
     ).astype(jnp.bfloat16)
     value_rows = projected[2]
-    gathered = lax.all_gather(queries, "pages", axis=0, tiled=True)
+    ring = [queries]
+    for hop in range(7):
+        ring.append(lax.ppermute(ring[-1], "pages", [(dev, (dev + 1) % 8) for dev in range(8)]))
+    gathered = jnp.roll(
+        jnp.concatenate(ring[::-1], axis=0),
+        (lax.axis_index("pages") + 1) * ring[0].shape[0],
+        axis=0,
+    )
     scores = (
         jnp.einsum(
             "qhd,khd->hqk",

time: 207 us -> 239 us (1.15)
  waiting for transfers between devices: 106 us -> 127 us
  local copies, waits for them, and re-layouts: 14.4 us -> 25.8 us
    ppermute x0 -> x7, waiting for transfers between devices: none -> 32.7 us  [shards_heads(): lax.ppermute(ring[-1], 'pages', [(dev, (dev + 1) % 8) for dev in range(8)])]
    all_gather x1 -> x0, waiting for transfers between devices: 11.8 us -> none  [shards_heads(): gathered = lax.all_gather(queries, 'pages', axis=0, tiled=True)]
    unnamed x20 -> x53, local copies, waits for them, and re-layouts: 2.24 us -> 13.4 us
  transfers between devices with their start and end apart: 4 -> 10, of which waited for: 4 -> 9; matrix products, arithmetic and copies ran while one was open for 16% -> 14% of each run, Pallas kernels for 0% -> 0%
where the time goes in v1:
time: 239 us; the launch traced here: 238 us
  waiting for transfers between devices  127 us (53%)
  matrix products  35.4 us (15%)
  local copies, waits for them, and re-layouts  25.8 us (11%)
  blocking collectives  17.9 us (7%)
  other arithmetic  17 us (7%)
  between operations  13.6 us (6%)
    reduce_scatter x2, waiting for transfers between devices, shards_heads(): lax.psum_scatter((summed.reshape(row_count, local_width), weight_sum), 'p...  63.8 us
    ppermute x7, waiting for transfers between devices, shards_heads(): lax.ppermute(ring[-1], 'pages', [(dev, (dev + 1) % 8) for dev in range(8)])  32.7 us
    reduce_scatter x1, waiting for transfers between devices, shards_heads(): lax.psum_scatter(jnp.dot(hidden, w_down, preferred_element_type=jnp.float...  30.6 us
    all_gather x1, blocking collectives, shards_heads(): attention = lax.all_gather(attention_local, 'mp', axis=1, tiled=True)  17.9 us
    unnamed x53, local copies, waits for them, and re-layouts  13.4 us
    dot_general x1, matrix products, shards_heads(): jnp.einsum('qhk,khd->qhd', prefix_weights.astype(jnp.bfloat16), value_hea...  12.5 us
    dot_general x1, matrix products, shards_heads(): jnp.einsum('qhd,khd->qhk', query_heads, key_heads, preferred_element_type...  10.8 us
  transfers between devices with their start and end apart: 10, of which 9 were waited for; matrix products, arithmetic and copies ran while one was open for 14% of the time, Pallas kernels for 0%

profile of v1, /device:TPU:0, one launch (start us, length us, event | category | flops | bytes accessed | tf_op | source)
XLA Modules:
  0.0 237.6 jit_solution(2204304393689355294)
XLA Ops:
  6.6 0.9 reduce_window_sum.11
  7.4 0.8 sub.41
  8.2 0.8 select_reduce_fusion.2
  9.0 1.3 fusion.9
  10.3 2.8 %fusion.16 = bf16[3,256,320]{1,2,0:T(8,128)(2,1)S(1)} fusion(bf16[3,1280,320]{1,2,0:T(8,128)(2,1)} %param.14, bf16[256,1280]{1,0:T(8,128)(2,1)} %param.13, f32[256]{0:T(256)S(1)} %add_rsqrt_fusion.5), kind=kOutput, calls=%fused_computation.29 | convolution fusion | flops 630374400 | bytes 3605504 | tf_op jit(solution)/shard_map/sd,jdc->jsc/dot_general | solution.py:252
  13.2 0.7 fusion.46
  13.9 0.2 multiply_cosine_fusion
  14.1 0.8 multiply_subtract_fusion
  15.0 0.8 fusion.33
  15.8 0.8 dynamic_slice.37
  16.5 1.1 fusion.30
  17.6 0.5 collective-permute-start
  18.1 0.1 fusion.44
  18.2 5.9 %collective-permute-done = bf16[256,320]{0,1:T(8,128)(2,1)} collective-permute-done((bf16[256,320]{0,1:T(8,128)(2,1)S(1)}, bf16[256,320]{0,1:T(8,128)(2,1)}, u32[]{:S(2)}, u32[]{:S(2)}) %collective-permute-start) | collective-permute-done | bytes 163872 | tf_op jit(solution)/shard_map/ppermute | solution.py:268
  24.2 0.2 select_reduce_fusion.3
  24.3 5.6 %collective-permute-done.1 = bf16[256,320]{0,1:T(8,128)(2,1)S(1)} collective-permute-done((bf16[256,320]{0,1:T(8,128)(2,1)}, bf16[256,320]{0,1:T(8,128)(2,1)S(1)}, u32[]{:S(2)}, u32[]{:S(2)}) %collective-permute-start.1) | collective-permute-done | bytes 163872 | tf_op jit(solution)/shard_map/ppermute | solution.py:268
  30.0 0.7 copy-done.5
  30.7 5.6 %collective-permute-done.2 = bf16[256,320]{0,1:T(8,128)(2,1)S(1)} collective-permute-done((bf16[256,320]{0,1:T(8,128)(2,1)S(1)}, bf16[256,320]{0,1:T(8,128)(2,1)S(1)}, u32[]{:S(2)}, u32[]{:S(2)}) %collective-permute-start.2) | collective-permute-done | bytes 163872 | tf_op jit(solution)/shard_map/ppermute | solution.py:268
  36.3 0.7 copy-done.7
  37.0 5.6 %collective-permute-done.3 = bf16[256,320]{0,1:T(8,128)(2,1)S(1)} collective-permute-done((bf16[256,320]{0,1:T(8,128)(2,1)S(1)}, bf16[256,320]{0,1:T(8,128)(2,1)S(1)}, u32[]{:S(2)}, u32[]{:S(2)}) %collective-permute-start.3) | collective-permute-done | bytes 163872 | tf_op jit(solution)/shard_map/ppermute | solution.py:268
  42.6 0.7 copy-done.9
  43.3 1.6 broadcast_compare_fusion
  44.9 4.1 %collective-permute-done.4 = bf16[256,320]{0,1:T(8,128)(2,1)} collective-permute-done((bf16[256,320]{0,1:T(8,128)(2,1)S(1)}, bf16[256,320]{0,1:T(8,128)(2,1)}, u32[]{:S(2)}, u32[]{:S(2)}) %collective-permute-start.4) | collective-permute-done | bytes 163872 | tf_op jit(solution)/shard_map/ppermute | solution.py:268
  49.0 2.4 %constant_dynamic-slice_fusion.1 = (bf16[4,128,320]{2,1,0:T(8,128)(2,1)}, bf16[4,128,320]{2,1,0:T(8,128)(2,1)}) fusion(bf16[4,128,1280]{2,1,0:T(8,128)(2,1)} %param.21, s32[]{:T(128)S(6)} %select_n.78, bf16[4,128,1280]{2,1,0:T(8,128)(2,1)} %param.22), kind=kLoop, calls=%fused_computation.107 | loop fusion | bytes 1310724 | tf_op jit(solution)/shard_map/dynamic_slice | solution.py:303
  51.5 1.9 copy.39
  53.4 2.1 copy.35
  55.5 2.2 reshape.336
  57.7 1.9 copy.33
  59.6 1.9 reshape_reshape.3
  61.5 1.2 multiply_reduce_fusion.2
  62.8 5.8 %collective-permute-done.6 = bf16[256,320]{0,1:T(8,128)(2,1)S(1)} collective-permute-done((bf16[256,320]{0,1:T(8,128)(2,1)}, bf16[256,320]{0,1:T(8,128)(2,1)S(1)}, u32[]{:S(2)}, u32[]{:S(2)}) %collective-permute-start.6) | collective-permute-done | bytes 163872 | tf_op jit(solution)/shard_map/ppermute | solution.py:268
  68.6 0.9 constant_dynamic-update-slice_fusion.14
  69.5 0.9 constant_dynamic-update-slice_fusion.13
  70.5 0.9 constant_dynamic-update-slice_fusion.12
  71.4 0.9 constant_dynamic-update-slice_fusion.11
  72.4 0.9 constant_dynamic-update-slice_fusion.10
  73.3 0.9 constant_dynamic-update-slice_fusion.9
  74.3 1.1 constant_dynamic-update-slice_fusion.6
  75.3 0.9 constant_dynamic-update-slice_fusion.5
  76.4 0.9 constant_dynamic-update-slice_fusion.1
  77.3 0.1 constant_dynamic-slice_fusion
  77.5 10.8 %fusion = (f32[2048,5]{0,1:T(8,128)}, f32[5,512,2048]{2,1,0:T(8,128)}) fusion(pred[2048,512]{0,1:T(8,128)(4,1)S(1)} %copy-done.3, bf16[2048,5,64]{0,2,1:T(8,128)(2,1)S(1)} %bitcast.85, f32[512,5,64]{0,2,1:T(8,128)S(1)} %copy-done.4, f32[5,64]{1,0:T(8,128)S(1)} %mul.318, f32[512,5]{0,1:T(8,128)S(1)} %add_rsqrt_fusion), kind=kOutput, calls=%fused_computation.1 | convolution fusion | flops 687298560 | bytes 24038656 | tf_op jit(solution)/shard_map/qhd,khd->qhk/dot_general | solution.py:318
  88.3 12.5 %fusion.2 = f32[5,64,2048]{2,1,0:T(8,128)} fusion(bf16[512,5,64]{0,2,1:T(8,128)(2,1)} %reshape_reshape.3, f32[5,512,2048]{2,1,0:T(8,128)} %get-tuple-element.24, pred[2048,512]{0,1:T(8,128)(4,1)} %broadcast_compare_fusion), kind=kOutput, calls=%fused_computation.3 | convolution fusion | flops 686817280 | bytes 24969216 | tf_op jit(solution)/shard_map/qhk,khd->qhd/dot_general | solution.py:324
  100.8 0.2 reduce-scatter.8.cloned.1.call-start
  101.1 0.6 copy-done.11
  101.7 1.0 multiply_reduce_fusion.5
  102.8 0.2 and_and_fusion
  103.0 2.4 %fusion.47 = (f32[5,256]{1,0:T(8,128)S(1)}, bf16[5,256,256]{1,2,0:T(8,128)(2,1)}) fusion(f32[256,5,32]{0,2,1:T(8,128)} %get-tuple-element.16, f32[256,5,32]{0,2,1:T(8,128)S(1)} %copy-done.11, f32[256,5]{0,1:T(8,128)S(1)} %add_rsqrt_fusion.1, f32[5,64]{1,0:T(8,128)S(1)} %mul.318, f32[256,5,64]{0,2,1:T(8,128)} %fusion.33, pred[256,256]{0,1:T(8,128)(4,1)S(1)} %and_and_fusion), kind=kOutput, calls=%fused_computation.132 | convolution fusion | flops 43744000 | bytes 1387776 | tf_op jit(solution)/shard_map/qhd,khd->hqk/dot_general | solution.py:275
  105.4 17.2 %reduce-scatter.6.cloned.1.call-done = f32[256,5]{0,1:T(8,128)} async-done(((f32[2048,5]{0,1:T(8,128)}), f32[256,5]{0,1:T(8,128)}) %reduce-scatter.6.cloned.1.call-update) | async-done | bytes 5136 | tf_op jit(solution)/shard_map/reduce_scatter | solution.py:330
  122.6 0.7 fusion.37
  123.3 46.7 %reduce-scatter.4.cloned.1.call-done = f32[256,320]{0,1:T(8,128)} async-done(((f32[2048,320]{0,1:T(8,128)}), f32[256,320]{0,1:T(8,128)}) %reduce-scatter.4.cloned.1.call-update) | async-done | bytes 327696 | tf_op jit(solution)/shard_map/reduce_scatter | solution.py:330
  170.0 1.6 fusion.19
  171.6 17.9 %all_gather.3 = bf16[256,1280]{0,1:T(8,128)(2,1)S(1)} all-gather(bf16[256,320]{0,1:T(8,128)(2,1)S(1)} %bitcast.88), channel_id=1, replica_groups=mesh['pages'=8,'mp'=4] {'mp'}, dimensions={1}, use_global_device_ids=true | all-gather | bytes 819200 | tf_op jit(solution)/shard_map/all_gather | solution.py:341
  189.5 1.1 multiply_reduce_fusion.1
  190.7 0.5 multiply_reduce_fusion
  191.2 0.4 multiply_convert_fusion
  191.6 1.9 convolution_bitcast_fusion
  193.5 0.3 copy-done.14
  193.8 2.3 fusion.20
  196.1 0.1 fusion.39
  196.2 30.6 %reduce-scatter.8.cloned.1.call-done = f32[64,1280]{1,0:T(8,128)} async-done(((f32[256,1280]{1,0:T(8,128)}), f32[64,1280]{1,0:T(8,128)}) %reduce-scatter.8.cloned.1.call-update) | async-done | bytes 327696 | tf_op jit(solution)/shard_map/reduce_scatter | solution.py:353
  226.8 1.1 multiply_reduce_fusion.4
  227.9 1.3 multiply_reduce_fusion.3
  229.2 1.9 multiply_convert_fusion.3
  (75 shorter events, 0.8 us)
Async XLA Ops:
  6.5 183.0 %copy-start = (bf16[1280,1280]{1,0:T(8,128)(2,1)S(1)}, bf16[1280,1280]{1,0:T(8,128)(2,1)}, u32[]{:S(2)}) copy-start(bf16[1280,1280]{1,0:T(8,128)(2,1)} %param.15) | copy-start | bytes 9830404
  6.5 116.1 %reduce-scatter.6.cloned.1.call-start = ((), (), s32[]{:S(2)}) async-start(), calls=%async_computation.4 | async-start | bytes 73728 | tf_op jit(solution)/shard_map/reduce_scatter | solution.py:330
  13.2 11.0 %copy-start.15 = (s32[32]{0:T(128)S(1)}, s32[32]{0:T(128)}, u32[]{:S(2)}) copy-start(s32[32]{0:T(128)} %param.23) | copy-start | bytes 388
  17.6 6.5 %collective-permute-start = (bf16[256,320]{0,1:T(8,128)(2,1)S(1)}, bf16[256,320]{0,1:T(8,128)(2,1)}, u32[]{:S(2)}, u32[]{:S(2)}) collective-permute-start(bf16[256,320]{0,1:T(8,128)(2,1)S(1)} %fusion.30), channel_id=1, source_target_pairs={{0,4},{4,8},{8,12},{12,16},{16,20},{20,24},{24,28},{28,0},{1,5},{5... | collective-permute-start | bytes 491528 | tf_op jit(solution)/shard_map/ppermute | solution.py:268
  24.1 5.9 %collective-permute-start.1 = (bf16[256,320]{0,1:T(8,128)(2,1)}, bf16[256,320]{0,1:T(8,128)(2,1)S(1)}, u32[]{:S(2)}, u32[]{:S(2)}) collective-permute-start(bf16[256,320]{0,1:T(8,128)(2,1)} %collective-permute-done), channel_id=1, source_target_pairs={{0,4},{4,8},{8,12},{12,16},{16,20},{20,24},{24,28},{28,0},{1,5},{5... | collective-permute-start | bytes 491528 | tf_op jit(solution)/shard_map/ppermute | solution.py:268
  30.0 0.7 copy-start.5
  30.7 5.6 %collective-permute-start.2 = (bf16[256,320]{0,1:T(8,128)(2,1)S(1)}, bf16[256,320]{0,1:T(8,128)(2,1)S(1)}, u32[]{:S(2)}, u32[]{:S(2)}) collective-permute-start(bf16[256,320]{0,1:T(8,128)(2,1)S(1)} %collective-permute-done.1), channel_id=1, source_target_pairs={{0,4},{4,8},{8,12},{12,16},{16,20},{20,24},{24,28},{28,0},{1,5},{5... | collective-permute-start | bytes 491528 | tf_op jit(solution)/shard_map/ppermute | solution.py:268
  36.3 0.7 copy-start.7
  37.0 5.6 %collective-permute-start.3 = (bf16[256,320]{0,1:T(8,128)(2,1)S(1)}, bf16[256,320]{0,1:T(8,128)(2,1)S(1)}, u32[]{:S(2)}, u32[]{:S(2)}) collective-permute-start(bf16[256,320]{0,1:T(8,128)(2,1)S(1)} %collective-permute-done.2), channel_id=1, source_target_pairs={{0,4},{4,8},{8,12},{12,16},{16,20},{20,24},{24,28},{28,0},{1,5},{5... | collective-permute-start | bytes 491528 | tf_op jit(solution)/shard_map/ppermute | solution.py:268
  42.6 0.7 copy-start.9
  43.3 5.7 %collective-permute-start.4 = (bf16[256,320]{0,1:T(8,128)(2,1)S(1)}, bf16[256,320]{0,1:T(8,128)(2,1)}, u32[]{:S(2)}, u32[]{:S(2)}) collective-permute-start(bf16[256,320]{0,1:T(8,128)(2,1)S(1)} %collective-permute-done.3), channel_id=1, source_target_pairs={{0,4},{4,8},{8,12},{12,16},{16,20},{20,24},{24,28},{28,0},{1,5},{5... | collective-permute-start | bytes 491528 | tf_op jit(solution)/shard_map/ppermute | solution.py:268
  49.0 13.7 %collective-permute-start.5 = (bf16[256,320]{0,1:T(8,128)(2,1)}, bf16[256,320]{0,1:T(8,128)(2,1)}, u32[]{:S(2)}, u32[]{:S(2)}) collective-permute-start(bf16[256,320]{0,1:T(8,128)(2,1)} %collective-permute-done.4), channel_id=1, source_target_pairs={{0,4},{4,8},{8,12},{12,16},{16,20},{20,24},{24,28},{28,0},{1,5},{5... | collective-permute-start | bytes 491528 | tf_op jit(solution)/shard_map/ppermute | solution.py:268
  61.4 14.8 %copy-start.10 = (bf16[256,320]{0,1:T(8,128)(2,1)S(1)}, bf16[256,320]{0,1:T(8,128)(2,1)}, u32[]{:S(2)}) copy-start(bf16[256,320]{0,1:T(8,128)(2,1)} %copy-done.9) | copy-start | bytes 491524
  61.4 14.9 %copy-start.8 = (bf16[256,320]{0,1:T(8,128)(2,1)S(1)}, bf16[256,320]{0,1:T(8,128)(2,1)}, u32[]{:S(2)}) copy-start(bf16[256,320]{0,1:T(8,128)(2,1)} %copy-done.7) | copy-start | bytes 491524
  61.5 14.9 %copy-start.6 = (bf16[256,320]{0,1:T(8,128)(2,1)S(1)}, bf16[256,320]{0,1:T(8,128)(2,1)}, u32[]{:S(2)}) copy-start(bf16[256,320]{0,1:T(8,128)(2,1)} %copy-done.5) | copy-start | bytes 491524
  62.7 5.9 %collective-permute-start.6 = (bf16[256,320]{0,1:T(8,128)(2,1)}, bf16[256,320]{0,1:T(8,128)(2,1)S(1)}, u32[]{:S(2)}, u32[]{:S(2)}) collective-permute-start(bf16[256,320]{0,1:T(8,128)(2,1)} %collective-permute-done.5), channel_id=1, source_target_pairs={{0,4},{4,8},{8,12},{12,16},{16,20},{20,24},{24,28},{28,0},{1,5},{5... | collective-permute-start | bytes 491528 | tf_op jit(solution)/shard_map/ppermute | solution.py:268
  74.3 3.2 %copy-start.3 = (pred[2048,512]{0,1:T(8,128)(4,1)S(1)}, pred[2048,512]{0,1:T(8,128)(4,1)}, u32[]{:S(2)}) copy-start(pred[2048,512]{0,1:T(8,128)(4,1)} %broadcast_compare_fusion) | copy-start | bytes 3145732
  74.3 3.2 %copy-start.4 = (f32[512,5,64]{0,2,1:T(8,128)S(1)}, f32[512,5,64]{0,2,1:T(8,128)}, u32[]{:S(2)}) copy-start(f32[512,5,64]{0,2,1:T(8,128)} %reshape.336) | copy-start | bytes 1966084
  88.3 81.7 %reduce-scatter.4.cloned.1.call-start = ((), (), s32[]{:S(2)}) async-start(), calls=%async_computation.3 | async-start | bytes 2949120 | tf_op jit(solution)/shard_map/reduce_scatter | solution.py:330
  100.8 0.9 copy-start.11
  100.8 1.9 copy-start.12
  100.8 1.9 copy-start.13
  100.8 125.9 %reduce-scatter.8.cloned.1.call-start = ((), (), s32[]{:S(2)}) async-start(), calls=%async_computation.5 | async-start | bytes 1638400 | tf_op jit(solution)/shard_map/reduce_scatter | solution.py:353
  170.0 21.6 %slice-start = ((s8[6553600]{0:T(1024)(128)(4,1)}), s8[4194304]{0:T(1024)(128)(4,1)S(1)}, s32[]{:S(2)}) async-start(s8[6553600]{0:T(1024)(128)(4,1)} %bitcast.82), calls=%async_computation.6 | async-start | bytes 8388608
  189.5 1.1 copy-start.1
  189.5 2.1 slice-start.1
  191.6 1.9 copy-start.2
  191.6 2.2 copy-start.14
Sparse Core Ops, SparseCore 0:
  88.4 34.1 reduce-scatter.5
  126.3 43.6 reduce-scatter.3
  196.2 30.4 reduce-scatter.7
